TPU v7x, 256 devices: a whole 4x4x8 slice. The times are simulated.
256 devices in a mesh: row: 8 (over z), col: 32 (over y, x, core).
Axes of the slice: x: 4, y: 4, z: 8, core: 2. Of those that a mesh axis runs over, the one named last changes fastest.
Arguments:
- embeds: bfloat16 [24576, 768], P('col'), may hold values from -6 to 6
- labels: bfloat16 [24576, 1000], P('col'), may hold values from -6 to 6
- sharpness: float32 [24576], P('col'), may hold values from 0.5 to 100
- pattern: int32 [192, 16], P('col'), may hold values from 0 to 191, as said below
- mask_pos: int32 [24576, 50], P('col'), may hold values from 0 to 2047, as said below
Outputs:
- propagated: bfloat16 [24576, 1000], P('col', 'row')
Inputs may be any that keep to these rules, and one draw needn't show every extreme that they name: `pattern`: split the row blocks into runs of 6 and the slots into runs of 2; within one run of row blocks and one run of slots, ids that lie in the same run of 6 block ids are equal. `mask_pos`: the 50 positions of a row are distinct; position k * 128 + m names row m of the row block's k-th candidate block.
All inputs are finite; a program needn't handle non-finite values.
Results may differ from a plain program's by a relative error of at most 0.012.
Values may be sent and summed in bfloat16 or wider, within the bound.
No kernel may reach another device: no remote copies, remote signals or barrier semaphores. Data moves between devices by JAX's collectives and lax.ppermute only.
A program may use at most 128 MiB of HBM per device.

v0:
```python
import math
import jax
import jax.numpy as jnp
from jax import lax
from jax.sharding import PartitionSpec as P

BLOCK = 128
SLOTS = 16
CHUNKS = 4
mixing = 0.75
lowest_logit = -1e30


def body(embeds, labels, sharpness, pattern, mask_pos):
    rows_here, width = embeds.shape
    classes = labels.shape[1]
    n_col = lax.axis_size("col")
    n_row = lax.axis_size("row")
    row_pos = lax.axis_index("row")
    blocks_here = rows_here // BLOCK
    slots_here = SLOTS // n_row
    span = slots_here * BLOCK
    my_slots = lax.dynamic_slice_in_dim(pattern, row_pos * slots_here, slots_here, 1)
    owners = my_slots // blocks_here
    local_ids = my_slots % blocks_here
    peers = jnp.arange(n_col, dtype=jnp.int32)
    wanted = jnp.max(jnp.where(owners[..., None] == peers, local_ids[..., None], 0), axis=(0, 1))
    requested = lax.all_to_all(wanted, "col", split_axis=0, concat_axis=0, tiled=True)
    embedding_tiles = embeds.reshape(blocks_here, BLOCK, width)
    send_emb = embedding_tiles[requested]
    shifted = mask_pos - row_pos * span
    shifted = jnp.where((shifted >= 0) & (shifted < span), shifted, span)
    positions = jnp.arange(span, dtype=jnp.int32)
    in_mask = jnp.any(shifted[:, :, None] == positions[None, None, :], axis=1)
    in_mask = in_mask.reshape(blocks_here, BLOCK, span)

    def propagate_using(weight_matrix, fetched_lab):
        width_here = fetched_lab.shape[-1]
        candidate_ids = fetched_lab[owners].reshape(blocks_here, span, width_here)
        blended_rows = jnp.einsum(
            "tmg,tgh->tmh", weight_matrix, candidate_ids, preferred_element_type=jnp.float32
        )
        return blended_rows.reshape(rows_here, width_here)

    fetched_emb = lax.all_to_all(send_emb, "col", split_axis=0, concat_axis=0, tiled=True)
    candidate_ids = fetched_emb[owners].reshape(blocks_here, span, width)
    scores = jnp.einsum(
        "evg,erg->evr", embedding_tiles, candidate_ids, preferred_element_type=jnp.float32
    ) / math.sqrt(width)
    logits = scores * sharpness.reshape(blocks_here, BLOCK, 1)
    local_max = jnp.max(jnp.where(in_mask, logits, lowest_logit), axis=2)
    local_sum = jnp.sum(jnp.where(in_mask, jnp.exp(logits - local_max[..., None]), 0.0), axis=2)
    stats = lax.all_gather(jnp.stack([local_max, local_sum]), "row")
    top = jnp.max(stats[:, 0], axis=0)
    totals = jnp.sum(stats[:, 1] * jnp.exp(stats[:, 0] - top), axis=0)
    weight_matrix = jnp.where(
        in_mask, jnp.exp(logits - top[..., None]) / totals[..., None], 0.0
    ).astype(jnp.bfloat16)
    rows_dev = rows_here // n_row
    piece = classes // CHUNKS
    lab_chunks = labels.reshape(rows_here, CHUNKS, piece).transpose(1, 0, 2)
    fetched = []
    for k in range(CHUNKS):
        send_lab = lab_chunks[k].reshape(blocks_here, BLOCK, piece)[requested]
        fetched.append(lax.all_to_all(send_lab, "col", split_axis=0, concat_axis=0, tiled=True))
    sums = []
    for k in range(CHUNKS):
        partial_one = propagate_using(weight_matrix, fetched[k]).astype(jnp.bfloat16)
        if k > 0:
            partial_one, sums[k - 1] = lax.optimization_barrier((partial_one, sums[k - 1]))
        sums.append(lax.psum(partial_one, "row"))
    spreads = []
    for k in range(CHUNKS):
        summed = sums[k].astype(jnp.float32)
        spread = (mixing * summed + (1.0 - mixing) * lab_chunks[k].astype(jnp.float32)).astype(
            jnp.bfloat16
        )
        send_spread = spread.reshape(blocks_here, BLOCK, piece)[requested]
        spreads.append(lax.all_to_all(send_spread, "col", split_axis=0, concat_axis=0, tiled=True))
    shares = []
    for k in range(CHUNKS):
        partial_two = propagate_using(weight_matrix, spreads[k]).astype(jnp.bfloat16)
        if k > 0:
            partial_two, shares[k - 1] = lax.optimization_barrier((partial_two, shares[k - 1]))
        shares.append(lax.psum_scatter(partial_two, "row", scatter_dimension=0, tiled=True))
    outs = []
    for k in range(CHUNKS):
        seed_rows = lax.dynamic_slice_in_dim(lab_chunks[k], row_pos * rows_dev, rows_dev, 0)
        share = shares[k].astype(jnp.float32)
        outs.append(
            (mixing * share + (1.0 - mixing) * seed_rows.astype(jnp.float32)).astype(jnp.bfloat16)
        )
    mine = jnp.concatenate(outs, axis=1)
    return lax.all_to_all(mine, "row", split_axis=1, concat_axis=0, tiled=True)


def solution(mesh):
    placed = (P("col", None), P("col", None), P("col"), P("col", None), P("col", None))
    return jax.shard_map(
        body, mesh=mesh, in_specs=placed, out_specs=P("col", "row"), check_vma=False
    )
```

profile of v0, /device:TPU:4, one launch (start us, length us, event | category | flops | bytes accessed | tf_op | source)
XLA Modules:
  0.0 808.5 jit_solution(6084548880981616726)
XLA Ops:
  8.8 7.6 all-to-all-start
  16.4 1.8 reshape.139
  23.4 2.0 gather_fusion.6
  25.4 6.7 all-to-all-start.4
  33.3 2.0 gather_fusion.4
  35.3 23.3 %all-to-all-done.4 = bf16[32,128,250]{2,1,0:T(8,128)(2,1)} async-done(((bf16[32,128,250]{2,1,0:T(8,128)(2,1)}), bf16[32,128,250]{2,1,0:T(8,128)(2,1)}, u32[]{:S(2)}, u32[]{:S(2)}) %all-to-all-start.4) | async-done | bytes 2048032 | tf_op jit(solution)/shard_map/all_to_all | solution.py:65
  58.6 8.4 %all-to-all-start.3 = ((bf16[32,128,250]{2,1,0:T(8,128)(2,1)}), bf16[32,128,250]{2,1,0:T(8,128)(2,1)}, u32[]{:S(2)}, u32[]{:S(2)}) async-start(bf16[32,128,250]{2,1,0:T(8,128)(2,1)} %gather_fusion.4), calls=%async_computation.3 | async-start | bytes 4194304 | tf_op jit(solution)/shard_map/all_to_all | solution.py:65
  67.0 3.6 gather_fusion
  70.6 22.9 %all-to-all-done.3 = bf16[32,128,250]{2,1,0:T(8,128)(2,1)} async-done(((bf16[32,128,250]{2,1,0:T(8,128)(2,1)}), bf16[32,128,250]{2,1,0:T(8,128)(2,1)}, u32[]{:S(2)}, u32[]{:S(2)}) %all-to-all-start.3) | async-done | bytes 2048032 | tf_op jit(solution)/shard_map/all_to_all | solution.py:65
  93.5 8.5 %all-to-all-start.1 = ((bf16[32,128,768]{2,1,0:T(8,128)(2,1)}), bf16[32,128,768]{2,1,0:T(8,128)(2,1)}, u32[]{:S(2)}, u32[]{:S(2)}) async-start(bf16[32,128,768]{2,1,0:T(8,128)(2,1)} %gather_fusion), calls=%async_computation.1 | async-start | bytes 12582912 | tf_op jit(solution)/shard_map/all_to_all | solution.py:45
  103.2 2.0 gather_fusion.2
  105.2 70.4 %all-to-all-done.1 = bf16[32,128,768]{2,1,0:T(8,128)(2,1)} async-done(((bf16[32,128,768]{2,1,0:T(8,128)(2,1)}), bf16[32,128,768]{2,1,0:T(8,128)(2,1)}, u32[]{:S(2)}, u32[]{:S(2)}) %all-to-all-start.1) | async-done | bytes 6291488 | tf_op jit(solution)/shard_map/all_to_all | solution.py:45
  175.5 9.1 %all-to-all-start.2 = ((bf16[32,128,250]{2,1,0:T(8,128)(2,1)}), bf16[32,128,250]{2,1,0:T(8,128)(2,1)}, u32[]{:S(2)}, u32[]{:S(2)}) async-start(bf16[32,128,250]{2,1,0:T(8,128)(2,1)} %gather_fusion.2), calls=%async_computation.2 | async-start | bytes 4194304 | tf_op jit(solution)/shard_map/all_to_all | solution.py:65
  184.8 7.2 fusion
  193.1 2.1 gather_fusion.12
  195.2 3.1 gather_fusion.7
  198.3 5.0 gather_fusion.1
  203.4 7.8 all-to-all-done.2
  211.1 8.4 %all-to-all-start.7 = ((bf16[32,128,250]{2,1,0:T(8,128)(2,1)}), bf16[32,128,250]{2,1,0:T(8,128)(2,1)}, u32[]{:S(2)}, u32[]{:S(2)}) async-start(bf16[32,128,250]{2,1,0:T(8,128)(2,1)} %gather_fusion.12), calls=%async_computation.7 | async-start | bytes 4194304 | tf_op jit(solution)/shard_map/all_to_all | solution.py:65
  219.6 2.5 select_reduce_fusion.1
  222.3 28.4 %all-gather = f32[16,6,128]{2,1,0:T(8,128)S(1)} all-gather(f32[2,6,128]{2,1,0:T(8,128)S(1)} %pad_maximum_fusion.1), channel_id=2, replica_groups=mesh['row'=8,'col'=32] {'row'}, dimensions={0}, use_global_device_ids=true | all-gather | bytes 55296 | tf_op jit(solution)/shard_map/all_gather | solution.py:53
  252.2 2.2 gather_fusion.5
  254.7 70.1 %all-reduce.5.cloned.1.call-done = bf16[768,250]{0,1:T(8,128)(2,1)} async-done(((bf16[768,250]{0,1:T(8,128)(2,1)}), bf16[768,250]{0,1:T(8,128)(2,1)}) %all-reduce.5.cloned.1.call-update) | async-done | bytes 384016 | tf_op jit(solution)/shard_map/psum | solution.py:71
  325.8 2.2 gather_fusion.3
  328.4 70.6 %all-reduce.7.cloned.1.call-done = bf16[768,250]{0,1:T(8,128)(2,1)} async-done(((bf16[768,250]{0,1:T(8,128)(2,1)}), bf16[768,250]{0,1:T(8,128)(2,1)}) %all-reduce.7.cloned.1.call-update) | async-done | bytes 384016 | tf_op jit(solution)/shard_map/psum | solution.py:71
  400.0 2.2 gather_fusion.13
  402.5 70.6 %all-reduce.9.cloned.1.call-done = bf16[768,250]{0,1:T(8,128)(2,1)} async-done(((bf16[768,250]{0,1:T(8,128)(2,1)}), bf16[768,250]{0,1:T(8,128)(2,1)}) %all-reduce.9.cloned.1.call-update) | async-done | bytes 384016 | tf_op jit(solution)/shard_map/psum | solution.py:71
  474.1 73.1 %all-reduce.11.cloned.1.call-done = bf16[768,250]{0,1:T(8,128)(2,1)} async-done(((bf16[768,250]{0,1:T(8,128)(2,1)}), bf16[768,250]{0,1:T(8,128)(2,1)}) %all-reduce.11.cloned.1.call-update) | async-done | bytes 384016 | tf_op jit(solution)/shard_map/psum | solution.py:71
  547.2 2.8 fusion.4
  551.2 2.0 gather_fusion.10
  553.2 7.6 all-to-all-start.6
  561.0 2.0 gather_fusion.8
  563.0 24.2 %all-to-all-done.6 = bf16[32,128,250]{2,1,0:T(8,128)(2,1)} async-done(((bf16[32,128,250]{2,1,0:T(8,128)(2,1)}), bf16[32,128,250]{2,1,0:T(8,128)(2,1)}, u32[]{:S(2)}, u32[]{:S(2)}) %all-to-all-start.6) | async-done | bytes 2048032 | tf_op jit(solution)/shard_map/all_to_all | solution.py:79
  587.2 8.3 %all-to-all-start.5 = ((bf16[32,128,250]{2,1,0:T(8,128)(2,1)}), bf16[32,128,250]{2,1,0:T(8,128)(2,1)}, u32[]{:S(2)}, u32[]{:S(2)}) async-start(bf16[32,128,250]{2,1,0:T(8,128)(2,1)} %gather_fusion.8), calls=%async_computation.5 | async-start | bytes 4194304 | tf_op jit(solution)/shard_map/all_to_all | solution.py:79
  595.7 2.0 gather_fusion.14
  597.7 24.3 %all-to-all-done.5 = bf16[32,128,250]{2,1,0:T(8,128)(2,1)} async-done(((bf16[32,128,250]{2,1,0:T(8,128)(2,1)}), bf16[32,128,250]{2,1,0:T(8,128)(2,1)}, u32[]{:S(2)}, u32[]{:S(2)}) %all-to-all-start.5) | async-done | bytes 2048032 | tf_op jit(solution)/shard_map/all_to_all | solution.py:79
  622.0 8.4 %all-to-all-start.8 = ((bf16[32,128,250]{2,1,0:T(8,128)(2,1)}), bf16[32,128,250]{2,1,0:T(8,128)(2,1)}, u32[]{:S(2)}, u32[]{:S(2)}) async-start(bf16[32,128,250]{2,1,0:T(8,128)(2,1)} %gather_fusion.14), calls=%async_computation.8 | async-start | bytes 4194304 | tf_op jit(solution)/shard_map/all_to_all | solution.py:79
  630.4 2.2 gather_fusion.11
  633.9 2.0 gather_fusion.16
  635.9 20.9 %all-to-all-done.8 = bf16[32,128,250]{2,1,0:T(8,128)(2,1)} async-done(((bf16[32,128,250]{2,1,0:T(8,128)(2,1)}), bf16[32,128,250]{2,1,0:T(8,128)(2,1)}, u32[]{:S(2)}, u32[]{:S(2)}) %all-to-all-start.8) | async-done | bytes 2048032 | tf_op jit(solution)/shard_map/all_to_all | solution.py:79
  656.9 8.3 %all-to-all-start.9 = ((bf16[32,128,250]{2,1,0:T(8,128)(2,1)}), bf16[32,128,250]{2,1,0:T(8,128)(2,1)}, u32[]{:S(2)}, u32[]{:S(2)}) async-start(bf16[32,128,250]{2,1,0:T(8,128)(2,1)} %gather_fusion.16), calls=%async_computation.9 | async-start | bytes 4194304 | tf_op jit(solution)/shard_map/all_to_all | solution.py:79
  665.3 2.2 gather_fusion.9
  670.8 2.2 gather_fusion.15
  674.1 34.3 %reduce-scatter.15.cloned.1.call-done = bf16[96,250]{1,0:T(8,128)(2,1)} async-done(((bf16[768,250]{1,0:T(8,128)(2,1)}), bf16[96,250]{1,0:T(8,128)(2,1)}) %reduce-scatter.15.cloned.1.call-update) | async-done | bytes 48016
  709.4 2.2 gather_fusion.17
  712.6 34.4 %reduce-scatter.17.cloned.1.call-done = bf16[96,250]{1,0:T(8,128)(2,1)} async-done(((bf16[768,250]{1,0:T(8,128)(2,1)}), bf16[96,250]{1,0:T(8,128)(2,1)}) %reduce-scatter.17.cloned.1.call-update) | async-done | bytes 48016
  751.0 34.6 %reduce-scatter.19.cloned.1.call-done = bf16[96,250]{1,0:T(8,128)(2,1)} async-done(((bf16[768,250]{1,0:T(8,128)(2,1)}), bf16[96,250]{1,0:T(8,128)(2,1)}) %reduce-scatter.19.cloned.1.call-update) | async-done | bytes 48016
  787.0 14.0 %all_to_all.76 = bf16[96,8,125]{2,0,1:T(8,128)(2,1)S(1)} all-to-all(bf16[96,8,125]{2,0,1:T(8,128)(2,1)S(1)} %copy.203), channel_id=1, replica_groups=mesh['row'=8,'col'=32] {'row'}, dimensions={1} | all-to-all | bytes 384000 | tf_op jit(solution)/shard_map/all_to_all | solution.py:94
  (87 shorter events, 31.9 us)
Async XLA Ops:
  6.5 60.5 %copy-start = (bf16[768,768]{1,0:T(8,128)(2,1)S(1)}, bf16[768,768]{1,0:T(8,128)(2,1)}, u32[]{:S(2)}) copy-start(bf16[768,768]{1,0:T(8,128)(2,1)} %param.5) | copy-start | bytes 3538948
  8.8 12.8 %all-to-all-start = ((s32[32,1,1]{2,1,0:T(1,128)}), s32[32,1,1]{2,1,0:T(1,128)S(1)}, u32[]{:S(2)}, u32[]{:S(2)}) async-start(s32[32,1,1]{2,1,0:T(1,128)} %copy.173), calls=%async_computation | async-start | bytes 32768 | tf_op jit(solution)/shard_map/all_to_all | solution.py:28
  25.4 33.2 %all-to-all-start.4 = ((bf16[32,128,250]{2,1,0:T(8,128)(2,1)}), bf16[32,128,250]{2,1,0:T(8,128)(2,1)}, u32[]{:S(2)}, u32[]{:S(2)}) async-start(bf16[32,128,250]{2,1,0:T(8,128)(2,1)} %gather_fusion.6), calls=%async_computation.4 | async-start | bytes 4194304 | tf_op jit(solution)/shard_map/all_to_all | solution.py:65
  58.6 34.9 %all-to-all-start.3 = ((bf16[32,128,250]{2,1,0:T(8,128)(2,1)}), bf16[32,128,250]{2,1,0:T(8,128)(2,1)}, u32[]{:S(2)}, u32[]{:S(2)}) async-start(bf16[32,128,250]{2,1,0:T(8,128)(2,1)} %gather_fusion.4), calls=%async_computation.3 | async-start | bytes 4194304 | tf_op jit(solution)/shard_map/all_to_all | solution.py:65
  93.5 82.0 %all-to-all-start.1 = ((bf16[32,128,768]{2,1,0:T(8,128)(2,1)}), bf16[32,128,768]{2,1,0:T(8,128)(2,1)}, u32[]{:S(2)}, u32[]{:S(2)}) async-start(bf16[32,128,768]{2,1,0:T(8,128)(2,1)} %gather_fusion), calls=%async_computation.1 | async-start | bytes 12582912 | tf_op jit(solution)/shard_map/all_to_all | solution.py:45
  105.2 79.5 %copy-start.7 = (s32[6,2]{1,0:T(8,128)S(1)}, s32[6,2]{1,0:T(8,128)}, u32[]{:S(2)}) copy-start(s32[6,2]{1,0:T(8,128)} %get-tuple-element.29) | copy-start | bytes 148
  105.2 79.6 %copy-start.6 = (s32[768,50]{0,1:T(8,128)S(1)}, s32[768,50]{0,1:T(8,128)}, u32[]{:S(2)}) copy-start(s32[768,50]{0,1:T(8,128)} %param.9) | copy-start | bytes 460804
  105.2 88.0 %copy-start.8 = (f32[768]{0:T(1024)S(1)}, f32[768]{0:T(1024)}, u32[]{:S(2)}) copy-start(f32[768]{0:T(1024)} %param.7) | copy-start | bytes 9220
  175.5 35.6 %all-to-all-start.2 = ((bf16[32,128,250]{2,1,0:T(8,128)(2,1)}), bf16[32,128,250]{2,1,0:T(8,128)(2,1)}, u32[]{:S(2)}, u32[]{:S(2)}) async-start(bf16[32,128,250]{2,1,0:T(8,128)(2,1)} %gather_fusion.2), calls=%async_computation.2 | async-start | bytes 4194304 | tf_op jit(solution)/shard_map/all_to_all | solution.py:65
  203.4 16.2 %copy-start.3 = (pred[6,128,256]{1,2,0:T(32,128)(4,1)S(1)}, pred[6,128,256]{1,2,0:T(32,128)(4,1)}, u32[]{:S(2)}) copy-start(pred[6,128,256]{1,2,0:T(32,128)(4,1)} %copy.177) | copy-start | bytes 589828
  211.1 188.9 %all-to-all-start.7 = ((bf16[32,128,250]{2,1,0:T(8,128)(2,1)}), bf16[32,128,250]{2,1,0:T(8,128)(2,1)}, u32[]{:S(2)}, u32[]{:S(2)}) async-start(bf16[32,128,250]{2,1,0:T(8,128)(2,1)} %gather_fusion.12), calls=%async_computation.7 | async-start | bytes 4194304 | tf_op jit(solution)/shard_map/all_to_all | solution.py:65
  219.5 105.3 %all-reduce.5.cloned.1.call-start = ((), (), s32[]{:S(2)}) async-start(), calls=%async_computation.15 | async-start | bytes 786432 | tf_op jit(solution)/shard_map/psum | solution.py:71
  219.6 31.1 %copy-start.4 = (pred[6,128,256]{1,2,0:T(32,128)(4,1)S(1)}, pred[6,128,256]{1,2,0:T(32,128)(4,1)}, u32[]{:S(2)}) copy-start(pred[6,128,256]{1,2,0:T(32,128)(4,1)} %copy.177) | copy-start | bytes 589828
  222.1 28.8 %copy-start.2 = (bf16[12,128,250]{2,1,0:T(8,128)(2,1)S(1)}, bf16[12,128,250]{2,1,0:T(8,128)(2,1)}, u32[]{:S(2)}) copy-start(bf16[12,128,250]{2,1,0:T(8,128)(2,1)} %gather_fusion.7) | copy-start | bytes 2304004
  252.2 146.8 %all-reduce.7.cloned.1.call-start = ((), (), s32[]{:S(2)}) async-start(), calls=%async_computation.16 | async-start | bytes 786432 | tf_op jit(solution)/shard_map/psum | solution.py:71
  325.8 147.4 %all-reduce.9.cloned.1.call-start = ((), (), s32[]{:S(2)}) async-start(), calls=%async_computation.17 | async-start | bytes 786432 | tf_op jit(solution)/shard_map/psum | solution.py:71
  400.0 147.2 %all-reduce.11.cloned.1.call-start = ((), (), s32[]{:S(2)}) async-start(), calls=%async_computation.18 | async-start | bytes 786432 | tf_op jit(solution)/shard_map/psum | solution.py:71
  553.2 7.6 copy-start.5
  553.2 34.0 %all-to-all-start.6 = ((bf16[32,128,250]{2,1,0:T(8,128)(2,1)}), bf16[32,128,250]{2,1,0:T(8,128)(2,1)}, u32[]{:S(2)}, u32[]{:S(2)}) async-start(bf16[32,128,250]{2,1,0:T(8,128)(2,1)} %gather_fusion.10), calls=%async_computation.6 | async-start | bytes 4194304 | tf_op jit(solution)/shard_map/all_to_all | solution.py:79
  587.2 34.8 %all-to-all-start.5 = ((bf16[32,128,250]{2,1,0:T(8,128)(2,1)}), bf16[32,128,250]{2,1,0:T(8,128)(2,1)}, u32[]{:S(2)}, u32[]{:S(2)}) async-start(bf16[32,128,250]{2,1,0:T(8,128)(2,1)} %gather_fusion.8), calls=%async_computation.5 | async-start | bytes 4194304 | tf_op jit(solution)/shard_map/all_to_all | solution.py:79
  622.0 34.8 %all-to-all-start.8 = ((bf16[32,128,250]{2,1,0:T(8,128)(2,1)}), bf16[32,128,250]{2,1,0:T(8,128)(2,1)}, u32[]{:S(2)}, u32[]{:S(2)}) async-start(bf16[32,128,250]{2,1,0:T(8,128)(2,1)} %gather_fusion.14), calls=%async_computation.8 | async-start | bytes 4194304 | tf_op jit(solution)/shard_map/all_to_all | solution.py:79
  630.4 39.4 %reduce-scatter.13.cloned.1.call-start = ((), (), s32[]{:S(2)}) async-start(), calls=%async_computation.19 | async-start | bytes 442368
  656.9 52.5 %all-to-all-start.9 = ((bf16[32,128,250]{2,1,0:T(8,128)(2,1)}), bf16[32,128,250]{2,1,0:T(8,128)(2,1)}, u32[]{:S(2)}, u32[]{:S(2)}) async-start(bf16[32,128,250]{2,1,0:T(8,128)(2,1)} %gather_fusion.16), calls=%async_computation.9 | async-start | bytes 4194304 | tf_op jit(solution)/shard_map/all_to_all | solution.py:79
  665.2 43.1 %reduce-scatter.15.cloned.1.call-start = ((), (), s32[]{:S(2)}) async-start(), calls=%async_computation.20 | async-start | bytes 442368
  670.8 76.3 %reduce-scatter.17.cloned.1.call-start = ((), (), s32[]{:S(2)}) async-start(), calls=%async_computation.21 | async-start | bytes 442368
  709.3 76.3 %reduce-scatter.19.cloned.1.call-start = ((), (), s32[]{:S(2)}) async-start(), calls=%async_computation.22 | async-start | bytes 442368
  711.6 90.1 %copy-start.1 = (bf16[768,768]{1,0:T(8,128)(2,1)S(1)}, bf16[768,768]{1,0:T(8,128)(2,1)}, u32[]{:S(2)}) copy-start(bf16[768,768]{1,0:T(8,128)(2,1)} %param.5) | copy-start | bytes 3538948
Sparse Core Ops, SparseCore 0:
  252.3 72.5 all-reduce.4
  327.2 71.7 all-reduce.6
  401.3 71.8 all-reduce.8
  475.4 71.8 all-reduce.10
  633.8 35.9 reduce-scatter.12
  672.2 36.1 reduce-scatter.14
  710.9 36.1 reduce-scatter.16
  749.5 36.0 reduce-scatter.18
where the time goes:
time: 810 us; the launch traced here: 809 us
  waiting for transfers between devices  584 us (72%)
  starting transfers between devices  81.6 us (10%)
  local copies, waits for them, and re-layouts  61.3 us (8%)
  blocking collectives  42.4 us (5%)
  other arithmetic  17.1 us (2%)
  between operations  13.9 us (2%)
    psum x4, waiting for transfers between devices, body(): sums.append(lax.psum(partial_one, 'row'))  284 us
    unnamed x12, waiting for transfers between devices  105 us
    all_to_all x1, waiting for transfers between devices, body(): lax.all_to_all(send_emb, 'col', split_axis=0, concat_axis=0, tiled=True)  70.4 us
    all_to_all x4, waiting for transfers between devices, body(): lax.all_to_all(send_spread, 'col', split_axis=0, concat_axis=0, tiled=True)  69.5 us
    all_to_all x4, waiting for transfers between devices, body(): lax.all_to_all(send_lab, 'col', split_axis=0, concat_axis=0, tiled=True)  54 us
    all_to_all x4, starting transfers between devices, body(): lax.all_to_all(send_spread, 'col', split_axis=0, concat_axis=0, tiled=True)  32.6 us
    all_to_all x4, starting transfers between devices, body(): lax.all_to_all(send_lab, 'col', split_axis=0, concat_axis=0, tiled=True)  32.5 us
    all_gather x1, blocking collectives, body(): stats = lax.all_gather(jnp.stack([local_max, local_sum]), 'row')  28.4 us
  transfers between devices with their start and end apart: 18, of which 16 were waited for; matrix products, arithmetic and copies ran while one was open for 9% of the time, Pallas kernels for 0%

commit v1 on v0

--- a/solution.py
+++ b/solution.py
@@ -68,7 +68,7 @@
         partial_one = propagate_using(weight_matrix, fetched[k]).astype(jnp.bfloat16)
         if k > 0:
             partial_one, sums[k - 1] = lax.optimization_barrier((partial_one, sums[k - 1]))
-        sums.append(lax.psum(partial_one, "row"))
+        sums.append(jnp.sum(lax.all_gather(partial_one, "row"), axis=0))
     spreads = []
     for k in range(CHUNKS):
         summed = sums[k].astype(jnp.float32)

time: 810 us -> 583 us (0.72)
  waiting for transfers between devices: 584 us -> 274 us
  blocking collectives: 42.4 us -> 146 us
  starting transfers between devices: 81.6 us -> 56.1 us
    psum x4 -> x0, waiting for transfers between devices: 284 us -> none  [body(): sums.append(lax.psum(partial_one, 'row'))]
    all_to_all x0 -> x3, blocking collectives: none -> 104 us  [body(): lax.all_to_all(send_lab, 'col', split_axis=0, concat_axis=0, tiled=True)]
    reduce_scatter x0 -> x1, waiting for transfers between devices: none -> 35.8 us  [body(): lax.psum_scatter(partial_two, 'row', scatter_dimension=0, tiled=True)]
    all_to_all x4 -> x1, waiting for transfers between devices: 54 us -> 22.8 us  [body(): lax.all_to_all(send_lab, 'col', split_axis=0, concat_axis=0, tiled=True)]
    unnamed x12 -> x11, waiting for transfers between devices: 105 us -> 74 us
    all_to_all x4 -> x1, starting transfers between devices: 32.5 us -> 7.11 us  [body(): lax.all_to_all(send_lab, 'col', split_axis=0, concat_axis=0, tiled=True)]
    all_gather x0 -> x4, waiting for transfers between devices: none -> 12 us  [body(): sums.append(jnp.sum(lax.all_gather(partial_one, 'row'), axis=0))]
    reduce_sum x0 -> x4, other arithmetic: none -> 11.8 us  [body(): sums.append(jnp.sum(lax.all_gather(partial_one, 'row'), axis=0))]
  transfers between devices with their start and end apart: 18 -> 15, of which waited for: 16 -> 13; matrix products, arithmetic and copies ran while one was open for 9% -> 10% of each run, Pallas kernels for 0% -> 0%
where the time goes in v1:
time: 583 us; the launch traced here: 581 us
  waiting for transfers between devices  274 us (47%)
  blocking collectives  146 us (25%)
  starting transfers between devices  56.1 us (10%)
  local copies, waits for them, and re-layouts  54.1 us (9%)
  other arithmetic  24.2 us (4%)
  between operations  13.9 us (2%)
  matrix products  12.2 us (2%)
    all_to_all x3, blocking collectives, body(): lax.all_to_all(send_lab, 'col', split_axis=0, concat_axis=0, tiled=True)  104 us
    unnamed x11, waiting for transfers between devices  74 us
    all_to_all x4, waiting for transfers between devices, body(): lax.all_to_all(send_spread, 'col', split_axis=0, concat_axis=0, tiled=True)  66.6 us
    all_to_all x1, waiting for transfers between devices, body(): lax.all_to_all(send_emb, 'col', split_axis=0, concat_axis=0, tiled=True)  62.8 us
    reduce_scatter x1, waiting for transfers between devices, body(): lax.psum_scatter(partial_two, 'row', scatter_dimension=0, tiled=True)  35.8 us
    all_to_all x4, starting transfers between devices, body(): lax.all_to_all(send_spread, 'col', split_axis=0, concat_axis=0, tiled=True)  32.7 us
    all_gather x1, blocking collectives, body(): stats = lax.all_gather(jnp.stack([local_max, local_sum]), 'row')  28.3 us
    all_to_all x1, waiting for transfers between devices, body(): lax.all_to_all(send_lab, 'col', split_axis=0, concat_axis=0, tiled=True)  22.8 us
  transfers between devices with their start and end apart: 15, of which 13 were waited for; matrix products, arithmetic and copies ran while one was open for 10% of the time, Pallas kernels for 0%

profile of v1, /device:TPU:4, one launch (start us, length us, event | category | flops | bytes accessed | tf_op | source)
XLA Modules:
  0.0 580.8 jit_solution(7901876910142957053)
XLA Ops:
  8.2 7.6 %all-to-all-start = ((s32[32,1,1]{2,1,0:T(1,128)}), s32[32,1,1]{2,1,0:T(1,128)S(1)}, u32[]{:S(2)}, u32[]{:S(2)}) async-start(s32[32,1,1]{2,1,0:T(1,128)} %copy.145), calls=%async_computation | async-start | bytes 32768 | tf_op jit(solution)/shard_map/all_to_all | solution.py:28
  21.7 2.0 gather_fusion.6
  23.7 7.1 %all-to-all-start.4 = ((bf16[32,128,250]{2,1,0:T(8,128)(2,1)}), bf16[32,128,250]{2,1,0:T(8,128)(2,1)}, u32[]{:S(2)}, u32[]{:S(2)}) async-start(bf16[32,128,250]{2,1,0:T(8,128)(2,1)} %gather_fusion.6), calls=%async_computation.4 | async-start | bytes 4194304 | tf_op jit(solution)/shard_map/all_to_all | solution.py:65
  30.8 3.6 gather_fusion
  34.4 22.8 %all-to-all-done.4 = bf16[32,128,250]{2,1,0:T(8,128)(2,1)} async-done(((bf16[32,128,250]{2,1,0:T(8,128)(2,1)}), bf16[32,128,250]{2,1,0:T(8,128)(2,1)}, u32[]{:S(2)}, u32[]{:S(2)}) %all-to-all-start.4) | async-done | bytes 2048032 | tf_op jit(solution)/shard_map/all_to_all | solution.py:65
  57.2 8.5 %all-to-all-start.1 = ((bf16[32,128,768]{2,1,0:T(8,128)(2,1)}), bf16[32,128,768]{2,1,0:T(8,128)(2,1)}, u32[]{:S(2)}, u32[]{:S(2)}) async-start(bf16[32,128,768]{2,1,0:T(8,128)(2,1)} %gather_fusion), calls=%async_computation.1 | async-start | bytes 12582912 | tf_op jit(solution)/shard_map/all_to_all | solution.py:45
  65.8 7.2 %fusion = pred[768,256]{1,0:T(8,128)(4,1)S(1)} fusion(s32[768,50]{0,1:T(8,128)S(1)} %and_select_fusion), kind=kLoop, calls=%fused_computation.19 | loop fusion | flops 19464192 | bytes 350208 | tf_op jit(solution)/shard_map/reduce_or | solution.py:34
  73.3 3.1 gather_fusion.7
  76.4 62.8 %all-to-all-done.1 = bf16[32,128,768]{2,1,0:T(8,128)(2,1)} async-done(((bf16[32,128,768]{2,1,0:T(8,128)(2,1)}), bf16[32,128,768]{2,1,0:T(8,128)(2,1)}, u32[]{:S(2)}, u32[]{:S(2)}) %all-to-all-start.1) | async-done | bytes 6291488 | tf_op jit(solution)/shard_map/all_to_all | solution.py:45
  139.2 5.0 gather_fusion.1
  144.2 2.4 select_reduce_fusion.1
  146.9 28.3 %all-gather = f32[16,6,128]{2,1,0:T(8,128)S(1)} all-gather(f32[2,6,128]{2,1,0:T(8,128)S(1)} %pad_maximum_fusion.1), channel_id=2, replica_groups=mesh['row'=8,'col'=32] {'row'}, dimensions={0}, use_global_device_ids=true | all-gather | bytes 55296 | tf_op jit(solution)/shard_map/all_gather | solution.py:53
  176.6 2.0 gather_fusion.4
  178.6 35.7 %all_to_all.76 = bf16[32,128,250]{2,1,0:T(8,128)(2,1)} all-to-all(bf16[32,128,250]{2,1,0:T(8,128)(2,1)} %gather_fusion.4), channel_id=1, replica_groups=mesh['row'=8,'col'=32] {'col'}, dimensions={0} | all-to-all | bytes 4096000 | tf_op jit(solution)/shard_map/all_to_all | solution.py:65
  214.3 2.2 gather_fusion.5
  217.6 3.2 all-gather.9.cloned.1.call-done
  220.8 2.6 reduce_sum.68
  223.4 2.0 gather_fusion.2
  225.5 34.0 %all_to_all.77 = bf16[32,128,250]{2,1,0:T(8,128)(2,1)} all-to-all(bf16[32,128,250]{2,1,0:T(8,128)(2,1)} %gather_fusion.2), channel_id=1, replica_groups=mesh['row'=8,'col'=32] {'col'}, dimensions={0} | all-to-all | bytes 4096000 | tf_op jit(solution)/shard_map/all_to_all | solution.py:65
  259.5 2.2 gather_fusion.3
  262.8 4.4 all-gather.11.cloned.1.call-done
  267.2 3.3 reduce_sum.69
  270.5 2.0 gather_fusion.12
  272.5 34.0 %all_to_all.78 = bf16[32,128,250]{2,1,0:T(8,128)(2,1)} all-to-all(bf16[32,128,250]{2,1,0:T(8,128)(2,1)} %gather_fusion.12), channel_id=1, replica_groups=mesh['row'=8,'col'=32] {'col'}, dimensions={0} | all-to-all | bytes 4096000 | tf_op jit(solution)/shard_map/all_to_all | solution.py:65
  306.5 2.2 gather_fusion.13
  309.8 4.4 all-gather.13.cloned.1.call-done
  314.3 3.3 reduce_sum.70
  319.5 2.0 gather_fusion.10
  321.5 7.6 %all-to-all-start.6 = ((bf16[32,128,250]{2,1,0:T(8,128)(2,1)}), bf16[32,128,250]{2,1,0:T(8,128)(2,1)}, u32[]{:S(2)}, u32[]{:S(2)}) async-start(bf16[32,128,250]{2,1,0:T(8,128)(2,1)} %gather_fusion.10), calls=%async_computation.6 | async-start | bytes 4194304 | tf_op jit(solution)/shard_map/all_to_all | solution.py:79
  329.7 2.0 gather_fusion.8
  331.8 23.8 %all-to-all-done.6 = bf16[32,128,250]{2,1,0:T(8,128)(2,1)} async-done(((bf16[32,128,250]{2,1,0:T(8,128)(2,1)}), bf16[32,128,250]{2,1,0:T(8,128)(2,1)}, u32[]{:S(2)}, u32[]{:S(2)}) %all-to-all-start.6) | async-done | bytes 2048032 | tf_op jit(solution)/shard_map/all_to_all | solution.py:79
  355.5 8.3 %all-to-all-start.5 = ((bf16[32,128,250]{2,1,0:T(8,128)(2,1)}), bf16[32,128,250]{2,1,0:T(8,128)(2,1)}, u32[]{:S(2)}, u32[]{:S(2)}) async-start(bf16[32,128,250]{2,1,0:T(8,128)(2,1)} %gather_fusion.8), calls=%async_computation.5 | async-start | bytes 4194304 | tf_op jit(solution)/shard_map/all_to_all | solution.py:79
  363.9 2.0 gather_fusion.14
  365.9 24.5 %all-to-all-done.5 = bf16[32,128,250]{2,1,0:T(8,128)(2,1)} async-done(((bf16[32,128,250]{2,1,0:T(8,128)(2,1)}), bf16[32,128,250]{2,1,0:T(8,128)(2,1)}, u32[]{:S(2)}, u32[]{:S(2)}) %all-to-all-start.5) | async-done | bytes 2048032 | tf_op jit(solution)/shard_map/all_to_all | solution.py:79
  390.4 8.3 %all-to-all-start.8 = ((bf16[32,128,250]{2,1,0:T(8,128)(2,1)}), bf16[32,128,250]{2,1,0:T(8,128)(2,1)}, u32[]{:S(2)}, u32[]{:S(2)}) async-start(bf16[32,128,250]{2,1,0:T(8,128)(2,1)} %gather_fusion.14), calls=%async_computation.8 | async-start | bytes 4194304 | tf_op jit(solution)/shard_map/all_to_all | solution.py:79
  398.8 2.2 gather_fusion.11
  402.1 2.6 reduce_sum.71
  404.9 2.0 gather_fusion.16
  406.9 18.3 %all-to-all-done.8 = bf16[32,128,250]{2,1,0:T(8,128)(2,1)} async-done(((bf16[32,128,250]{2,1,0:T(8,128)(2,1)}), bf16[32,128,250]{2,1,0:T(8,128)(2,1)}, u32[]{:S(2)}, u32[]{:S(2)}) %all-to-all-start.8) | async-done | bytes 2048032 | tf_op jit(solution)/shard_map/all_to_all | solution.py:79
  425.2 8.3 %all-to-all-start.9 = ((bf16[32,128,250]{2,1,0:T(8,128)(2,1)}), bf16[32,128,250]{2,1,0:T(8,128)(2,1)}, u32[]{:S(2)}, u32[]{:S(2)}) async-start(bf16[32,128,250]{2,1,0:T(8,128)(2,1)} %gather_fusion.16), calls=%async_computation.9 | async-start | bytes 4194304 | tf_op jit(solution)/shard_map/all_to_all | solution.py:79
  433.6 2.2 gather_fusion.9
  439.3 2.2 gather_fusion.15
  442.5 34.3 %reduce-scatter.15.cloned.1.call-done = bf16[96,250]{1,0:T(8,128)(2,1)} async-done(((bf16[768,250]{1,0:T(8,128)(2,1)}), bf16[96,250]{1,0:T(8,128)(2,1)}) %reduce-scatter.15.cloned.1.call-update) | async-done | bytes 48016
  477.8 37.6 %reduce-scatter.17.cloned.1.call-done = bf16[96,250]{1,0:T(8,128)(2,1)} async-done(((bf16[768,250]{1,0:T(8,128)(2,1)}), bf16[96,250]{1,0:T(8,128)(2,1)}) %reduce-scatter.17.cloned.1.call-update) | async-done | bytes 48016
  516.3 3.1 gather_fusion.17
  519.5 2.3 convolution_convert_fusion
  522.2 35.8 %reduce-scatter.19.cloned.1.call-done = bf16[96,250]{1,0:T(8,128)(2,1)} async-done(((bf16[768,250]{1,0:T(8,128)(2,1)}), bf16[96,250]{1,0:T(8,128)(2,1)}) %reduce-scatter.19.cloned.1.call-update) | async-done | bytes 48016 | tf_op jit(solution)/shard_map/reduce_scatter | solution.py:85
  559.3 14.0 %all_to_all.79 = bf16[96,8,125]{2,0,1:T(8,128)(2,1)S(1)} all-to-all(bf16[96,8,125]{2,0,1:T(8,128)(2,1)S(1)} %copy.167), channel_id=1, replica_groups=mesh['row'=8,'col'=32] {'row'}, dimensions={1} | all-to-all | bytes 384000 | tf_op jit(solution)/shard_map/all_to_all | solution.py:94
  (72 shorter events, 25.3 us)
Async XLA Ops:
  6.5 24.3 %copy-start = (bf16[768,768]{1,0:T(8,128)(2,1)S(1)}, bf16[768,768]{1,0:T(8,128)(2,1)}, u32[]{:S(2)}) copy-start(bf16[768,768]{1,0:T(8,128)(2,1)} %param.5) | copy-start | bytes 3538948
  8.2 12.8 %all-to-all-start = ((s32[32,1,1]{2,1,0:T(1,128)}), s32[32,1,1]{2,1,0:T(1,128)S(1)}, u32[]{:S(2)}, u32[]{:S(2)}) async-start(s32[32,1,1]{2,1,0:T(1,128)} %copy.145), calls=%async_computation | async-start | bytes 32768 | tf_op jit(solution)/shard_map/all_to_all | solution.py:28
  23.7 33.5 %all-to-all-start.4 = ((bf16[32,128,250]{2,1,0:T(8,128)(2,1)}), bf16[32,128,250]{2,1,0:T(8,128)(2,1)}, u32[]{:S(2)}, u32[]{:S(2)}) async-start(bf16[32,128,250]{2,1,0:T(8,128)(2,1)} %gather_fusion.6), calls=%async_computation.4 | async-start | bytes 4194304 | tf_op jit(solution)/shard_map/all_to_all | solution.py:65
  34.4 31.4 %copy-start.3 = (s32[768,50]{0,1:T(8,128)S(1)}, s32[768,50]{0,1:T(8,128)}, u32[]{:S(2)}) copy-start(s32[768,50]{0,1:T(8,128)} %param.9) | copy-start | bytes 460804
  34.4 38.9 %copy-start.4 = (f32[768]{0:T(1024)S(1)}, f32[768]{0:T(1024)}, u32[]{:S(2)}) copy-start(f32[768]{0:T(1024)} %param.7) | copy-start | bytes 9220
  57.2 82.0 %all-to-all-start.1 = ((bf16[32,128,768]{2,1,0:T(8,128)(2,1)}), bf16[32,128,768]{2,1,0:T(8,128)(2,1)}, u32[]{:S(2)}, u32[]{:S(2)}) async-start(bf16[32,128,768]{2,1,0:T(8,128)(2,1)} %gather_fusion), calls=%async_computation.1 | async-start | bytes 12582912 | tf_op jit(solution)/shard_map/all_to_all | solution.py:45
  65.6 155.1 %all-gather.9.cloned.1.call-start = ((), (), s32[]{:S(2)}) async-start(), calls=%async_computation.15 | async-start | bytes 3538944 | tf_op jit(solution)/shard_map/all_gather | solution.py:71
  146.6 28.8 %copy-start.2 = (bf16[12,128,250]{2,1,0:T(8,128)(2,1)S(1)}, bf16[12,128,250]{2,1,0:T(8,128)(2,1)}, u32[]{:S(2)}) copy-start(bf16[12,128,250]{2,1,0:T(8,128)(2,1)} %gather_fusion.7) | copy-start | bytes 2304004
  176.6 90.6 %all-gather.11.cloned.1.call-start = ((), (), s32[]{:S(2)}) async-start(), calls=%async_computation.16 | async-start | bytes 3538944 | tf_op jit(solution)/shard_map/all_gather | solution.py:71
  223.4 90.9 %all-gather.13.cloned.1.call-start = ((), (), s32[]{:S(2)}) async-start(), calls=%async_computation.17 | async-start | bytes 3538944 | tf_op jit(solution)/shard_map/all_gather | solution.py:71
  321.5 34.0 %all-to-all-start.6 = ((bf16[32,128,250]{2,1,0:T(8,128)(2,1)}), bf16[32,128,250]{2,1,0:T(8,128)(2,1)}, u32[]{:S(2)}, u32[]{:S(2)}) async-start(bf16[32,128,250]{2,1,0:T(8,128)(2,1)} %gather_fusion.10), calls=%async_computation.6 | async-start | bytes 4194304 | tf_op jit(solution)/shard_map/all_to_all | solution.py:79
  329.1 72.9 %all-gather.15.cloned.1.call-start = ((), (), s32[]{:S(2)}) async-start(), calls=%async_computation.18 | async-start | bytes 3538944 | tf_op jit(solution)/shard_map/all_gather | solution.py:71
  355.5 34.8 %all-to-all-start.5 = ((bf16[32,128,250]{2,1,0:T(8,128)(2,1)}), bf16[32,128,250]{2,1,0:T(8,128)(2,1)}, u32[]{:S(2)}, u32[]{:S(2)}) async-start(bf16[32,128,250]{2,1,0:T(8,128)(2,1)} %gather_fusion.8), calls=%async_computation.5 | async-start | bytes 4194304 | tf_op jit(solution)/shard_map/all_to_all | solution.py:79
  390.4 34.8 %all-to-all-start.8 = ((bf16[32,128,250]{2,1,0:T(8,128)(2,1)}), bf16[32,128,250]{2,1,0:T(8,128)(2,1)}, u32[]{:S(2)}, u32[]{:S(2)}) async-start(bf16[32,128,250]{2,1,0:T(8,128)(2,1)} %gather_fusion.14), calls=%async_computation.8 | async-start | bytes 4194304 | tf_op jit(solution)/shard_map/all_to_all | solution.py:79
  398.7 39.6 %reduce-scatter.13.cloned.1.call-start = ((), (), s32[]{:S(2)}) async-start(), calls=%async_computation.19 | async-start | bytes 442368
  425.2 91.1 %all-to-all-start.9 = ((bf16[32,128,250]{2,1,0:T(8,128)(2,1)}), bf16[32,128,250]{2,1,0:T(8,128)(2,1)}, u32[]{:S(2)}, u32[]{:S(2)}) async-start(bf16[32,128,250]{2,1,0:T(8,128)(2,1)} %gather_fusion.16), calls=%async_computation.9 | async-start | bytes 4194304 | tf_op jit(solution)/shard_map/all_to_all | solution.py:79
  433.5 43.2 %reduce-scatter.15.cloned.1.call-start = ((), (), s32[]{:S(2)}) async-start(), calls=%async_computation.20 | async-start | bytes 442368
  439.2 76.2 %reduce-scatter.17.cloned.1.call-start = ((), (), s32[]{:S(2)}) async-start(), calls=%async_computation.21 | async-start | bytes 442368
  477.7 80.3 %reduce-scatter.19.cloned.1.call-start = ((), (), s32[]{:S(2)}) async-start(), calls=%async_computation.22 | async-start | bytes 442368 | tf_op jit(solution)/shard_map/reduce_scatter | solution.py:85
  519.5 54.5 %copy-start.1 = (bf16[768,768]{1,0:T(8,128)(2,1)S(1)}, bf16[768,768]{1,0:T(8,128)(2,1)}, u32[]{:S(2)}) copy-start(bf16[768,768]{1,0:T(8,128)(2,1)} %param.5) | copy-start | bytes 3538948
Sparse Core Ops, SparseCore 0:
  176.7 44.0 all-gather.8
  223.5 43.5 all-gather.10
  270.6 43.5 all-gather.12
  331.4 43.5 all-gather.14
  402.2 36.0 reduce-scatter.12
  440.6 36.1 reduce-scatter.14
  479.3 36.0 reduce-scatter.16
  521.9 36.0 reduce-scatter.18
